TPU v7x, 32 devices: a whole 2x2x4 slice. The times are simulated.
32 devices in a mesh: tm: 4 (over y, x), series: 8 (over z, core).
Axes of the slice: x: 2, y: 2, z: 4, core: 2. Of those that a mesh axis runs over, the one named last changes fastest.
Arguments:
- codes: int32 [8, 512], P(None, ('tm', 'series')), may hold values from 0 to 916478, as said below
- owner_slot: int32 [8], replicated, may hold values from 0 to 7, each once
- edges: int32 [4096], replicated, may hold values from 0 to 2096640, as said below
- w_in: bfloat16 [128, 2304], replicated, may hold values from -0.09375 to 0.09375
- w_dt: bfloat16 [128, 32], replicated, may hold values from -0.5 to 0.5
- dt_bias: float32 [32], replicated, may hold values from -1 to 1
- decay_rate: float32 [32], replicated, may hold values from 1e-05 to 0.1
- grad_out: bfloat16 [8, 512, 2048], P('series', 'tm'), may hold values from -6 to 6
Outputs:
- ssd_output: bfloat16 [8, 512, 2048], P('series', 'tm')
- grad_in: float32 [128, 2304], replicated
Inputs may be any that keep to these rules, and one draw needn't show every extreme that they name: `codes`: each row is one series in the order of ingestion slots. edges[0] is 0 and edges rise strictly.
All inputs are finite; a program needn't handle non-finite values.
Results may differ from a plain program's by a relative error of at most 0.0062.
The roundings to bfloat16 on the way count: a program that leaves them out, or rounds other values in their place, can miss the bound.
Values sent between devices are 32-bit elements; how exact they have to be, the bound alone decides.
No kernel may reach another device: no remote copies, remote signals or barrier semaphores. Data moves between devices by JAX's collectives and lax.ppermute only.
A program may use at most 128 MiB of HBM per device.

v0:
```python
import math
import jax
import jax.numpy as jnp
from jax import lax
from jax.sharding import PartitionSpec as P

code_ceiling = 2097152.0


def carried_in(array, axis, combine, identity, reverse):
    count, position = (lax.axis_size(axis), lax.axis_index(axis))
    everything = jax.tree.map(lambda part: lax.all_gather(part, axis), array)
    start = jax.tree.map(
        lambda part, zero: jnp.broadcast_to(jnp.asarray(zero, part.dtype), part.shape),
        array,
        identity,
    )

    def lap(k, before):
        at = count - 1 - k if reverse else k
        reached = at > position if reverse else at < position
        new = combine(before, jax.tree.map(lambda part: part[at], everything))
        return jax.tree.map(lambda a, b: jnp.where(reached, a, b), new, before)

    return lax.fori_loop(0, count, lap, start)


def decay_matrix(cum_decay):
    row_count = cum_decay.shape[0]
    causal = jnp.arange(row_count)[:, None] >= jnp.arange(row_count)[None, :]
    log_span = cum_decay.T[:, :, None] - cum_decay.T[:, None, :]
    return jnp.where(causal[None], jnp.exp(jnp.where(causal[None], log_span, -60.0)), 0.0)


def carry_combine(earlier, later):
    return (earlier[0] * later[0], later[0][:, None, None] * earlier[1] + later[1])


def on_device(codes, owner_slot, edges, w_in, w_dt, dt_bias, decay_rate, grad_out):
    fl = jnp.float32
    half = jnp.bfloat16
    tok_rows = grad_out.shape[1]
    head_count = dt_bias.shape[0]
    inner_width = grad_out.shape[2]
    head_dim = inner_width // head_count
    state_dim = (w_in.shape[1] - inner_width) // 2
    seq_len = tok_rows * lax.axis_size("tm")
    series_count = lax.axis_size("series")
    ordered = jnp.take(codes, owner_slot, axis=0).astype(fl)
    own_series = lax.all_to_all(ordered, "series", split_axis=0, concat_axis=1, tiled=True)
    reading = own_series[0]
    edge_float = edges.astype(fl)
    upper_edge = jnp.concatenate([edge_float[1:], jnp.full((1,), code_ceiling, fl)])
    onehot = (
        (edge_float[None, :] <= reading[:, None]) & (upper_edge[None, :] > reading[:, None])
    ).astype(fl)
    counts = lax.psum(jnp.sum(onehot, axis=0), "tm")
    before = jnp.cumsum(counts) - counts
    bin_table = jnp.stack([before, counts, edge_float, upper_edge - edge_float], axis=1)
    picked = jnp.dot(onehot, bin_table, precision=lax.Precision.HIGHEST)
    within_bin = (reading - picked[:, 2]) / picked[:, 3]
    quantile = (picked[:, 0] + picked[:, 1] * within_bin) / seq_len
    frequency = (jnp.arange(w_in.shape[0], dtype=fl) + 0.5) * math.pi
    features = jnp.cos(quantile[:, None] * frequency).astype(half)
    projected = jnp.dot(features, w_in, preferred_element_type=fl).astype(half)
    x_heads = projected[:, :inner_width].reshape(tok_rows, head_count, head_dim)
    b_proj = projected[:, inner_width : inner_width + state_dim]
    c_proj = projected[:, inner_width + state_dim :]
    step_size = jax.nn.softplus(dt_bias + jnp.dot(features, w_dt, preferred_element_type=fl))
    cum_decay = jnp.cumsum(-step_size * decay_rate, axis=0)
    tail_factor = jnp.exp(cum_decay[-1][None, :] - cum_decay) * step_size
    head_factor = jnp.exp(cum_decay)
    grad_heads = grad_out[0].reshape(tok_rows, head_count, head_dim)
    masked = decay_matrix(cum_decay) * step_size.T[:, None, :]
    scores = jnp.dot(c_proj, b_proj.T, preferred_element_type=fl)
    weights = (scores[None] * masked).astype(half)
    x_weighted = (x_heads * tail_factor[:, :, None]).astype(half)
    state_local = jnp.einsum("thp,tn->hpn", x_weighted, b_proj, preferred_element_type=fl)
    block_gate = jnp.exp(cum_decay[-1])
    grad_weighted = (grad_heads * head_factor[:, :, None]).astype(half)
    adjoint_local = jnp.einsum("thp,tn->hpn", grad_weighted, c_proj, preferred_element_type=fl)
    identity = (jnp.ones((head_count,), fl), jnp.zeros((head_count, head_dim, state_dim), fl))
    _, state_in = carried_in((block_gate, state_local), "tm", carry_combine, identity, False)
    _, adjoint_in = carried_in((block_gate, adjoint_local), "tm", carry_combine, identity, True)
    state_half = state_in.astype(half)
    adjoint_half = adjoint_in.astype(half)
    output = jnp.einsum("hts,shp->thp", weights, x_heads, preferred_element_type=fl)
    output = (
        output
        + jnp.einsum("tn,hpn->thp", c_proj, state_half, preferred_element_type=fl)
        * head_factor[:, :, None]
    )
    ssd_output = output.reshape(1, tok_rows, inner_width).astype(half)
    grad_x = jnp.einsum("hts,thp->shp", weights, grad_heads, preferred_element_type=fl)
    grad_x = (
        grad_x
        + jnp.einsum("sn,hpn->shp", b_proj, adjoint_half, preferred_element_type=fl)
        * tail_factor[:, :, None]
    )
    pair_scores = jnp.einsum("thp,shp->hts", grad_heads, x_heads, preferred_element_type=fl)
    pair_mixed = jnp.sum(pair_scores * masked, axis=0).astype(half)
    grad_b = jnp.dot(pair_mixed.T, c_proj, preferred_element_type=fl)
    grad_b = grad_b + jnp.einsum("shp,hpn->sn", x_weighted, adjoint_half, preferred_element_type=fl)
    grad_c = jnp.dot(pair_mixed, b_proj, preferred_element_type=fl)
    grad_c = grad_c + jnp.einsum(
        "thp,hpn->tn", grad_weighted, state_half, preferred_element_type=fl
    )
    grad_rows = jnp.concatenate(
        [
            grad_x.reshape(tok_rows, inner_width).astype(half),
            grad_b.astype(half),
            grad_c.astype(half),
        ],
        axis=1,
    )
    local_grad = jnp.einsum("tf,tw->fw", features, grad_rows, preferred_element_type=fl)
    share_grad = lax.psum_scatter(local_grad, "series", scatter_dimension=1, tiled=True)
    share_grad = lax.psum(share_grad, "tm")
    total_grad = lax.all_gather(share_grad, "series", axis=1, tiled=True)
    grad_in = total_grad / math.sqrt(series_count * seq_len)
    return (ssd_output, grad_in)


def solution(mesh):
    return jax.shard_map(
        on_device,
        mesh=mesh,
        in_specs=(P(None, ("tm", "series")), P(), P(), P(), P(), P(), P(), P("series", "tm", None)),
        out_specs=(P("series", "tm", None), P()),
        check_vma=False,
    )
```

profile of v0, /device:TPU:0, one launch (start us, length us, event | category | flops | bytes accessed | tf_op | source)
XLA Modules:
  0.0 267.1 jit_solution(18337310911339434361)
XLA Ops:
  10.5 6.3 %all-to-all-start = ((f32[8,1,16]{2,1,0:T(1,128)}), f32[8,1,16]{2,1,0:T(1,128)S(1)}, u32[]{:S(2)}, u32[]{:S(2)}) async-start(f32[8,1,16]{2,1,0:T(1,128)} %bitcast.1), calls=%async_computation | async-start | bytes 8192 | tf_op jit(solution)/shard_map/all_to_all | solution.py:50
  19.8 2.5 all-to-all-done
  24.0 16.0 %psum.14 = f32[4096]{0:T(1024)S(1)} all-reduce(f32[4096]{0:T(1024)S(1)} %convert_reduce_fusion), channel_id=1, replica_groups=mesh['tm'=4,'series'=8] {'tm'}, use_global_device_ids=true, to_apply=%region_1.2 | all-reduce | flops 4096 | bytes 32768 | tf_op jit(solution)/shard_map/psum | solution.py:57
  46.9 7.0 %all-gather.2 = f32[4,1,32]{2,1,0:T(1,128)S(1)} all-gather(f32[1,1,32]{2,1,0:T(1,128)S(1)} %get-tuple-element.295), channel_id=1, replica_groups=mesh['tm'=4,'series'=8] {'tm'}, dimensions={0}, use_global_device_ids=true | all-gather | bytes 640 | tf_op jit(solution)/shard_map/all_gather | solution.py:12
  54.8 2.6 fusion.2
  59.3 2.3 convolution_bitcast_fusion
  61.6 33.1 %all-gather.11.cloned.1.call-done = f32[128,64,128]{2,1,0:T(8,128)} async-done(((f32[32,64,128]{2,1,0:T(8,128)}), f32[128,64,128]{2,1,0:T(8,128)}) %all-gather.11.cloned.1.call-update) | async-done | bytes 4194320 | tf_op jit(solution)/shard_map/all_gather | solution.py:12
  94.7 6.0 %while.31 = (s32[]{:T(128)}, f32[32,64,128]{2,1,0:T(8,128)S(1)}, s32[]{:T(128)}, f32[4,32]{1,0:T(4,128)S(1)}, f32[4,32,64,128]{3,2,1,0:T(8,128)}, /*index=5*/s32[]{:T(128)}, s32[]{:T(128)}, s32[]{:T(128)}, s32[]{:T(128)}) while((s32[]{:T(128)}, f32[32,64,128]{2,1,0:T(8,128)S(1)}, s32[]{:T(128)}, f32[4,32]{1,0:T(4,128)S(1)}, ...), condition=%wide.region_8.9_spmd.clone, body=%wide.region_7.8_spmd.clone.sunk | while | flops 1048584 | bytes 3146279 | solution.py:25
  94.7 1.5 fusion.79
  96.2 1.5 fusion.79
  97.7 1.5 fusion.79
  99.3 1.5 fusion.79
  100.7 1.5 fusion.10
  102.3 1.9 fusion.7
  104.1 45.2 %all-gather.9.cloned.1.call-done = f32[128,64,128]{2,1,0:T(8,128)} async-done(((f32[32,64,128]{2,1,0:T(8,128)}), f32[128,64,128]{2,1,0:T(8,128)}) %all-gather.9.cloned.1.call-update) | async-done | bytes 4194320 | tf_op jit(solution)/shard_map/all_gather | solution.py:12
  149.3 6.0 %while.30 = (s32[]{:T(128)}, f32[32,64,128]{2,1,0:T(8,128)S(1)}, s32[]{:T(128)}, f32[4,32]{1,0:T(4,128)S(1)}, f32[4,32,64,128]{3,2,1,0:T(8,128)}, /*index=5*/s32[]{:T(128)}, s32[]{:T(128)}) while((s32[]{:T(128)}, f32[32,64,128]{2,1,0:T(8,128)S(1)}, s32[]{:T(128)}, f32[4,32]{1,0:T(4,128)S(1)}, f32[4,32,64,128]{3,2,1,0:T(8,128)}, ...), condition=%wide.region_6.7_spmd.clone, body=%wide.region_5.6_spmd.clone.sunk | while | flops 1048580 | bytes 3146217 | solution.py:25
  149.3 1.5 fusion.78
  150.9 1.5 fusion.78
  152.4 1.5 fusion.78
  153.9 1.5 fusion.78
  155.7 1.6 fusion.15
  157.4 32.7 %reduce-scatter.2.cloned.1.call-done = f32[128,288]{0,1:T(8,128)} async-done(((f32[128,2304]{0,1:T(8,128)}), f32[128,288]{0,1:T(8,128)}) %reduce-scatter.2.cloned.1.call-update) | async-done | bytes 147472 | tf_op jit(solution)/shard_map/reduce_scatter | solution.py:117
  190.1 43.2 %all-reduce.2.cloned.1.call-done = f32[128,288]{0,1:T(8,128)} async-done(((f32[128,288]{0,1:T(8,128)}), f32[128,288]{0,1:T(8,128)}) %all-reduce.2.cloned.1.call-update) | async-done | bytes 147472 | tf_op jit(solution)/shard_map/psum | solution.py:118
  236.8 21.0 %all-gather.7.cloned.1.call-done = f32[128,2304]{0,1:T(8,128)} async-done(((f32[128,288]{0,1:T(8,128)}), f32[128,2304]{0,1:T(8,128)}) %all-gather.7.cloned.1.call-update) | async-done | bytes 1179664 | tf_op jit(solution)/shard_map/all_gather | solution.py:119
  (85 shorter events, 24.1 us)
Async XLA Ops:
  7.2 34.8 %copy-start = (bf16[128,2304]{1,0:T(8,128)(2,1)S(1)}, bf16[128,2304]{1,0:T(8,128)(2,1)}, u32[]{:S(2)}) copy-start(bf16[128,2304]{1,0:T(8,128)(2,1)} %param.15) | copy-start | bytes 1769476
  10.5 11.8 %all-to-all-start = ((f32[8,1,16]{2,1,0:T(1,128)}), f32[8,1,16]{2,1,0:T(1,128)S(1)}, u32[]{:S(2)}, u32[]{:S(2)}) async-start(f32[8,1,16]{2,1,0:T(1,128)} %bitcast.1), calls=%async_computation | async-start | bytes 8192 | tf_op jit(solution)/shard_map/all_to_all | solution.py:50
  16.8 77.9 %all-gather.11.cloned.1.call-start = ((), (), s32[]{:S(2)}) async-start(), calls=%async_computation.6 | async-start | bytes 5242880 | tf_op jit(solution)/shard_map/all_gather | solution.py:12
  18.5 24.1 %copy-start.7 = (bf16[128,32]{0,1:T(8,128)(2,1)S(1)}, bf16[128,32]{0,1:T(8,128)(2,1)}, u32[]{:S(2)}) copy-start(bf16[128,32]{0,1:T(8,128)(2,1)} %param.16) | copy-start | bytes 24580
  18.5 24.1 %copy-start.8 = (f32[32]{0:T(128)S(1)}, f32[32]{0:T(128)}, u32[]{:S(2)}) copy-start(f32[32]{0:T(128)} %param.17) | copy-start | bytes 388
  18.5 24.6 %copy-start.6 = (f32[32]{0:T(128)S(1)}, f32[32]{0:T(128)}, u32[]{:S(2)}) copy-start(f32[32]{0:T(128)} %param.18) | copy-start | bytes 388
  42.6 2.7 %copy-start.3 = (bf16[128,2304]{1,0:T(8,128)(2,1)}, bf16[128,2304]{1,0:T(8,128)(2,1)S(1)}, u32[]{:S(2)}) copy-start(bf16[128,2304]{1,0:T(8,128)(2,1)S(1)} %convolution_convert_fusion) | copy-start | bytes 1769476
  44.8 104.5 %all-gather.9.cloned.1.call-start = ((), (), s32[]{:S(2)}) async-start(), calls=%async_computation.5 | async-start | bytes 5242880 | tf_op jit(solution)/shard_map/all_gather | solution.py:12
  45.2 1.5 copy-start.1
  46.7 143.3 %reduce-scatter.2.cloned.1.call-start = ((), (), s32[]{:S(2)}) async-start(), calls=%async_computation.2 | async-start | bytes 1327104 | tf_op jit(solution)/shard_map/reduce_scatter | solution.py:117
  100.7 1.5 copy-start.5
  149.3 6.4 %copy-start.4 = (bf16[128,32,64]{0,2,1:T(8,128)(2,1)S(1)}, bf16[128,32,64]{0,2,1:T(8,128)(2,1)}, u32[]{:S(2)}) copy-start(bf16[128,32,64]{0,2,1:T(8,128)(2,1)} %fusion.7) | copy-start | bytes 1572868
  155.3 78.0 %copy-start.2 = (bf16[128,2048]{0,1:T(8,128)(2,1)S(1)}, bf16[128,2048]{0,1:T(8,128)(2,1)}, u32[]{:S(2)}) copy-start(bf16[128,2048]{0,1:T(8,128)(2,1)} %copy-done.1) | copy-start | bytes 1572868
  157.3 76.0 %all-reduce.2.cloned.1.call-start = ((), (), s32[]{:S(2)}) async-start(), calls=%async_computation.3 | async-start | bytes 294912 | tf_op jit(solution)/shard_map/psum | solution.py:118
  190.1 67.7 %all-gather.7.cloned.1.call-start = ((), (), s32[]{:S(2)}) async-start(), calls=%async_computation.4 | async-start | bytes 1327104 | tf_op jit(solution)/shard_map/all_gather | solution.py:119
Sparse Core Ops, SparseCore 0:
  44.9 49.7 all-gather.10
  96.6 52.6 all-gather.8
  157.4 32.5 reduce-scatter.1
  192.8 40.4 all-reduce.1
  234.9 22.8 all-gather.6
where the time goes:
time: 268 us; the launch traced here: 267 us
  waiting for transfers between devices  178 us (66%)
  blocking collectives  23 us (9%)
  matrix products  20.3 us (8%)
  other arithmetic  18.5 us (7%)
  between operations  14.1 us (5%)
  local copies, waits for them, and re-layouts  6.62 us (2%)
  starting transfers between devices  6.53 us (2%)
    all_gather x2, waiting for transfers between devices, carried_in(): everything = jax.tree.map(lambda part: lax.all_gather(part, axis), array)  78.3 us
    psum x1, waiting for transfers between devices, on_device(): share_grad = lax.psum(share_grad, 'tm')  43.2 us
    reduce_scatter x1, waiting for transfers between devices, on_device(): lax.psum_scatter(local_grad, 'series', scatter_dimension=1, tiled=True)  32.7 us
    all_gather x1, waiting for transfers between devices, on_device(): total_grad = lax.all_gather(share_grad, 'series', axis=1, tiled=True)  21 us
    psum x1, blocking collectives, on_device(): counts = lax.psum(jnp.sum(onehot, axis=0), 'tm')  16 us
    select_n x8, other arithmetic, lap(): return jax.tree.map(lambda a, b: jnp.where(reached, a, b), new, before)  11.7 us
    all_gather x1, blocking collectives, carried_in(): everything = jax.tree.map(lambda part: lax.all_gather(part, axis), array)  6.99 us
    all_to_all x1, starting transfers between devices, on_device(): lax.all_to_all(ordered, 'series', split_axis=0, concat_axis=1, tiled=True)  6.33 us
  transfers between devices with their start and end apart: 6, of which 6 were waited for; matrix products, arithmetic and copies ran while one was open for 9% of the time, Pallas kernels for 0%

commit v1 on v0

--- a/solution.py
+++ b/solution.py
@@ -115,7 +115,8 @@
     )
     local_grad = jnp.einsum("tf,tw->fw", features, grad_rows, preferred_element_type=fl)
     share_grad = lax.psum_scatter(local_grad, "series", scatter_dimension=1, tiled=True)
-    share_grad = lax.psum(share_grad, "tm")
+    pieces = lax.all_gather(share_grad, "tm", axis=0, tiled=False)
+    share_grad = pieces.sum(axis=0)
     total_grad = lax.all_gather(share_grad, "series", axis=1, tiled=True)
     grad_in = total_grad / math.sqrt(series_count * seq_len)
     return (ssd_output, grad_in)

time: 268 us -> 238 us (0.89)
  waiting for transfers between devices: 178 us -> 133 us
  blocking collectives: 23 us -> 36 us
    psum x1 -> x0, waiting for transfers between devices: 43.2 us -> none  [on_device(): share_grad = lax.psum(share_grad, 'tm')]
    all_gather x0 -> x1, blocking collectives: none -> 13 us  [on_device(): pieces = lax.all_gather(share_grad, 'tm', axis=0, tiled=False)]
  transfers between devices with their start and end apart: 6 -> 5, of which waited for: 6 -> 5; matrix products, arithmetic and copies ran while one was open for 9% -> 11% of each run, Pallas kernels for 0% -> 0%
where the time goes in v1:
time: 238 us; the launch traced here: 236 us
  waiting for transfers between devices  133 us (56%)
  blocking collectives  36 us (15%)
  matrix products  20.3 us (9%)
  other arithmetic  19.6 us (8%)
  between operations  14 us (6%)
  local copies, waits for them, and re-layouts  6.82 us (3%)
  starting transfers between devices  6.49 us (3%)
    all_gather x2, waiting for transfers between devices, carried_in(): everything = jax.tree.map(lambda part: lax.all_gather(part, axis), array)  78.3 us
    reduce_scatter x1, waiting for transfers between devices, on_device(): lax.psum_scatter(local_grad, 'series', scatter_dimension=1, tiled=True)  32.8 us
    all_gather x1, waiting for transfers between devices, on_device(): total_grad = lax.all_gather(share_grad, 'series', axis=1, tiled=True)  19.3 us
    psum x1, blocking collectives, on_device(): counts = lax.psum(jnp.sum(onehot, axis=0), 'tm')  16 us
    all_gather x1, blocking collectives, on_device(): pieces = lax.all_gather(share_grad, 'tm', axis=0, tiled=False)  13 us
    select_n x8, other arithmetic, lap(): return jax.tree.map(lambda a, b: jnp.where(reached, a, b), new, before)  11.7 us
    all_gather x1, blocking collectives, carried_in(): everything = jax.tree.map(lambda part: lax.all_gather(part, axis), array)  6.99 us
    all_to_all x1, starting transfers between devices, on_device(): lax.all_to_all(ordered, 'series', split_axis=0, concat_axis=1, tiled=True)  6.33 us
  transfers between devices with their start and end apart: 5, of which 5 were waited for; matrix products, arithmetic and copies ran while one was open for 11% of the time, Pallas kernels for 0%

profile of v1, /device:TPU:0, one launch (start us, length us, event | category | flops | bytes accessed | tf_op | source)
XLA Modules:
  0.0 236.4 jit_solution(3595886966155110359)
XLA Ops:
  10.5 6.3 %all-to-all-start = ((f32[8,1,16]{2,1,0:T(1,128)}), f32[8,1,16]{2,1,0:T(1,128)S(1)}, u32[]{:S(2)}, u32[]{:S(2)}) async-start(f32[8,1,16]{2,1,0:T(1,128)} %bitcast.1), calls=%async_computation | async-start | bytes 8192 | tf_op jit(solution)/shard_map/all_to_all | solution.py:50
  19.8 2.5 %all-to-all-done = f32[8,1,16]{2,1,0:T(1,128)S(1)} async-done(((f32[8,1,16]{2,1,0:T(1,128)}), f32[8,1,16]{2,1,0:T(1,128)S(1)}, u32[]{:S(2)}, u32[]{:S(2)}) %all-to-all-start) | async-done | bytes 544 | tf_op jit(solution)/shard_map/all_to_all | solution.py:50
  24.0 16.0 %psum.7 = f32[4096]{0:T(1024)S(1)} all-reduce(f32[4096]{0:T(1024)S(1)} %convert_reduce_fusion), channel_id=1, replica_groups=mesh['tm'=4,'series'=8] {'tm'}, use_global_device_ids=true, to_apply=%region_1.2 | all-reduce | flops 4096 | bytes 32768 | tf_op jit(solution)/shard_map/psum | solution.py:57
  46.9 7.0 %all-gather.3 = f32[4,1,32]{2,1,0:T(1,128)S(1)} all-gather(f32[1,1,32]{2,1,0:T(1,128)S(1)} %get-tuple-element.295), channel_id=1, replica_groups=mesh['tm'=4,'series'=8] {'tm'}, dimensions={0}, use_global_device_ids=true | all-gather | bytes 640 | tf_op jit(solution)/shard_map/all_gather | solution.py:12
  54.8 2.6 %fusion.2 = bf16[128,128]{0,1:T(8,128)(2,1)S(1)} fusion(bf16[128,32,64]{0,2,1:T(8,128)(2,1)} %bitcast.110, bf16[128,32,64]{0,2,1:T(8,128)(2,1)S(1)} %bitcast.106, f32[32,128]{1,0:T(8,128)S(1)} %get-tuple-element.298, f32[32,128]{1,0:T(8,128)S(1)} %copy.51, pred[128,128]{0,1:T(8,128)(4,1)S(1)} %iota_compare_fusion), kind=kOutput, calls=%fused_computation.9 | convolution fusion | flops 70238208 | bytes 1130496 | tf_op jit(solution)/shard_map/thp,shp->hts/dot_general | solution.py:100
  59.3 2.4 convolution_bitcast_fusion
  61.6 33.1 %all-gather.12.cloned.1.call-done = f32[128,64,128]{2,1,0:T(8,128)} async-done(((f32[32,64,128]{2,1,0:T(8,128)}), f32[128,64,128]{2,1,0:T(8,128)}) %all-gather.12.cloned.1.call-update) | async-done | bytes 4194320 | tf_op jit(solution)/shard_map/all_gather | solution.py:12
  94.7 6.0 %while.31 = (s32[]{:T(128)}, f32[32,64,128]{2,1,0:T(8,128)S(1)}, s32[]{:T(128)}, f32[4,32]{1,0:T(4,128)S(1)}, f32[4,32,64,128]{3,2,1,0:T(8,128)}, /*index=5*/s32[]{:T(128)}, s32[]{:T(128)}, s32[]{:T(128)}, s32[]{:T(128)}) while((s32[]{:T(128)}, f32[32,64,128]{2,1,0:T(8,128)S(1)}, s32[]{:T(128)}, f32[4,32]{1,0:T(4,128)S(1)}, ...), condition=%wide.region_8.9_spmd.clone, body=%wide.region_7.8_spmd.clone.sunk | while | flops 1048584 | bytes 3146279 | solution.py:25
  94.7 1.5 fusion.79
  96.2 1.5 fusion.79
  97.8 1.5 fusion.79
  99.3 1.5 fusion.79
  100.8 1.5 fusion.10
  102.3 1.9 fusion.7
  104.1 45.2 %all-gather.10.cloned.1.call-done = f32[128,64,128]{2,1,0:T(8,128)} async-done(((f32[32,64,128]{2,1,0:T(8,128)}), f32[128,64,128]{2,1,0:T(8,128)}) %all-gather.10.cloned.1.call-update) | async-done | bytes 4194320 | tf_op jit(solution)/shard_map/all_gather | solution.py:12
  149.3 6.0 %while.30 = (s32[]{:T(128)}, f32[32,64,128]{2,1,0:T(8,128)S(1)}, s32[]{:T(128)}, f32[4,32]{1,0:T(4,128)S(1)}, f32[4,32,64,128]{3,2,1,0:T(8,128)}, /*index=5*/s32[]{:T(128)}, s32[]{:T(128)}) while((s32[]{:T(128)}, f32[32,64,128]{2,1,0:T(8,128)S(1)}, s32[]{:T(128)}, f32[4,32]{1,0:T(4,128)S(1)}, f32[4,32,64,128]{3,2,1,0:T(8,128)}, ...), condition=%wide.region_6.7_spmd.clone, body=%wide.region_5.6_spmd.clone.sunk | while | flops 1048580 | bytes 3146217 | solution.py:25
  149.3 1.5 fusion.78
  150.9 1.5 fusion.78
  152.4 1.5 fusion.78
  153.9 1.5 fusion.78
  155.7 1.6 fusion.15
  157.4 32.8 %reduce-scatter.2.cloned.1.call-done = f32[128,288]{0,1:T(8,128)} async-done(((f32[128,2304]{0,1:T(8,128)}), f32[128,288]{0,1:T(8,128)}) %reduce-scatter.2.cloned.1.call-update) | async-done | bytes 147472 | tf_op jit(solution)/shard_map/reduce_scatter | solution.py:117
  190.2 13.0 %all-gather.2 = f32[512,288]{0,1:T(8,128)S(1)} all-gather(f32[128,288]{0,1:T(8,128)} %reduce-scatter.2.cloned.1.call-done), channel_id=4, replica_groups=mesh['tm'=4,'series'=8] {'tm'}, dimensions={0}, use_global_device_ids=true | all-gather | bytes 737280 | tf_op jit(solution)/shard_map/all_gather | solution.py:118
  207.8 19.3 %all-gather.8.cloned.1.call-done = f32[128,2304]{0,1:T(8,128)} async-done(((f32[128,288]{0,1:T(8,128)}), f32[128,2304]{0,1:T(8,128)}) %all-gather.8.cloned.1.call-update) | async-done | bytes 1179664 | tf_op jit(solution)/shard_map/all_gather | solution.py:120
  (85 shorter events, 25.3 us)
Async XLA Ops:
  7.2 34.8 %copy-start = (bf16[128,2304]{1,0:T(8,128)(2,1)S(1)}, bf16[128,2304]{1,0:T(8,128)(2,1)}, u32[]{:S(2)}) copy-start(bf16[128,2304]{1,0:T(8,128)(2,1)} %param.15) | copy-start | bytes 1769476
  10.5 11.8 %all-to-all-start = ((f32[8,1,16]{2,1,0:T(1,128)}), f32[8,1,16]{2,1,0:T(1,128)S(1)}, u32[]{:S(2)}, u32[]{:S(2)}) async-start(f32[8,1,16]{2,1,0:T(1,128)} %bitcast.1), calls=%async_computation | async-start | bytes 8192 | tf_op jit(solution)/shard_map/all_to_all | solution.py:50
  16.8 77.9 %all-gather.12.cloned.1.call-start = ((), (), s32[]{:S(2)}) async-start(), calls=%async_computation.5 | async-start | bytes 5242880 | tf_op jit(solution)/shard_map/all_gather | solution.py:12
  18.5 24.1 %copy-start.7 = (bf16[128,32]{0,1:T(8,128)(2,1)S(1)}, bf16[128,32]{0,1:T(8,128)(2,1)}, u32[]{:S(2)}) copy-start(bf16[128,32]{0,1:T(8,128)(2,1)} %param.16) | copy-start | bytes 24580
  18.5 24.1 %copy-start.8 = (f32[32]{0:T(128)S(1)}, f32[32]{0:T(128)}, u32[]{:S(2)}) copy-start(f32[32]{0:T(128)} %param.17) | copy-start | bytes 388
  18.5 24.6 %copy-start.6 = (f32[32]{0:T(128)S(1)}, f32[32]{0:T(128)}, u32[]{:S(2)}) copy-start(f32[32]{0:T(128)} %param.18) | copy-start | bytes 388
  42.6 2.7 %copy-start.3 = (bf16[128,2304]{1,0:T(8,128)(2,1)}, bf16[128,2304]{1,0:T(8,128)(2,1)S(1)}, u32[]{:S(2)}) copy-start(bf16[128,2304]{1,0:T(8,128)(2,1)S(1)} %convolution_convert_fusion) | copy-start | bytes 1769476
  44.8 104.5 %all-gather.10.cloned.1.call-start = ((), (), s32[]{:S(2)}) async-start(), calls=%async_computation.4 | async-start | bytes 5242880 | tf_op jit(solution)/shard_map/all_gather | solution.py:12
  45.2 1.6 copy-start.1
  46.7 143.5 %reduce-scatter.2.cloned.1.call-start = ((), (), s32[]{:S(2)}) async-start(), calls=%async_computation.2 | async-start | bytes 1327104 | tf_op jit(solution)/shard_map/reduce_scatter | solution.py:117
  100.7 1.5 copy-start.5
  149.3 6.4 %copy-start.4 = (bf16[128,32,64]{0,2,1:T(8,128)(2,1)S(1)}, bf16[128,32,64]{0,2,1:T(8,128)(2,1)}, u32[]{:S(2)}) copy-start(bf16[128,32,64]{0,2,1:T(8,128)(2,1)} %fusion.7) | copy-start | bytes 1572868
  157.3 47.1 %copy-start.2 = (bf16[128,2048]{0,1:T(8,128)(2,1)S(1)}, bf16[128,2048]{0,1:T(8,128)(2,1)}, u32[]{:S(2)}) copy-start(bf16[128,2048]{0,1:T(8,128)(2,1)} %copy-done.1) | copy-start | bytes 1572868
  157.3 69.8 %all-gather.8.cloned.1.call-start = ((), (), s32[]{:S(2)}) async-start(), calls=%async_computation.3 | async-start | bytes 1327104 | tf_op jit(solution)/shard_map/all_gather | solution.py:120
Sparse Core Ops, SparseCore 0:
  44.9 49.7 all-gather.11
  96.6 52.6 all-gather.9
  157.4 32.7 reduce-scatter.1
  204.6 22.5 all-gather.7
